TPU v7x, 32 devices: a whole 2x2x4 slice. The times are simulated.
32 devices in a mesh: seq: 8 (over y, x, core), ch: 4 (over z).
Axes of the slice: x: 2, y: 2, z: 4, core: 2. Of those that a mesh axis runs over, the one named last changes fastest.
Arguments:
- inputs: bfloat16 [4096, 2048], P('seq', 'ch'), may hold values from -6 to 6
- gate_in: float32 [2048], P('ch'), may hold values from 0.25 to 2
- gate_out: float32 [2048], P('ch'), may hold values from 0.25 to 2
- first_blocks: bfloat16 [8, 512, 512], P('seq'), may hold values from -0.25 to 0.25
- second_blocks: bfloat16 [512, 8, 8], P('seq'), may hold values from -2 to 2
- channel_blocks: bfloat16 [4, 512, 512], P('ch'), may hold values from -0.25 to 0.25
- group_mix: bfloat16 [512, 4, 4], replicated, may hold values from -3 to 3
- cotangent: bfloat16 [4096, 2048], P('seq', 'ch'), may hold values from -6 to 6
Outputs:
- outputs: bfloat16 [4096, 2048], P('seq', 'ch')
- input_grad: bfloat16 [4096, 2048], P('seq', 'ch')
- channel_grad: float32 [4, 512, 512], P('ch', 'seq')
- block_grad: float32 [8, 512, 512], P('seq', 'ch')
All inputs are finite; a program needn't handle non-finite values.
Results may differ from a plain program's by a relative error of at most 0.0072.
Values may be sent and summed in bfloat16 or wider, within the bound.
No kernel may reach another device: no remote copies, remote signals or barrier semaphores. Data moves between devices by JAX's collectives and lax.ppermute only.
A program may use at most 64 MiB of HBM per device.

v0:
```python
import jax
import jax.numpy as jnp
from jax import lax
from jax.sharding import PartitionSpec as P


def to_columns(values):
    return lax.all_to_all(values, "seq", split_axis=1, concat_axis=0, tiled=True)


def to_rows(values):
    return lax.all_to_all(values, "seq", split_axis=0, concat_axis=1, tiled=True)


def group_apply(blocks, table):
    owner = lax.axis_index("ch")
    narrow = blocks.shape[2] // lax.axis_size("ch")
    table_rows = lax.dynamic_slice_in_dim(table, owner * narrow, narrow, 0)
    mixed = jnp.einsum(
        "rgk,kgh->rhk",
        lax.all_to_all(blocks, "ch", split_axis=2, concat_axis=1, tiled=True),
        table_rows,
        preferred_element_type=jnp.float32,
    )
    return lax.all_to_all(mixed, "ch", split_axis=1, concat_axis=2, tiled=True)


def on_device(
    inputs, gate_in, gate_out, first_blocks, second_blocks, channel_blocks, group_mix, cotangent
):
    count_a = first_blocks.shape[0]
    length_q = first_blocks.shape[1]
    rows_local = inputs.shape[0]
    width_local = inputs.shape[1]
    groups_local = channel_blocks.shape[0]
    block_width = channel_blocks.shape[1]
    source = inputs.astype(jnp.float32).reshape(count_a, length_q, width_local)
    slope_in = jax.nn.sigmoid(gate_in * source)
    gated = (source * slope_in).astype(jnp.bfloat16)
    mixed_first = jnp.einsum(
        "acb,abd->acd", first_blocks, gated, preferred_element_type=jnp.float32
    ).astype(jnp.bfloat16)
    turned = to_columns(mixed_first)
    mixed_second = jnp.einsum(
        "cea,acd->ecd", second_blocks, turned, preferred_element_type=jnp.float32
    ).astype(jnp.bfloat16)
    returned = to_rows(mixed_second).astype(jnp.float32)
    slope_out = jax.nn.sigmoid(gate_out * source)
    hidden = (source + returned * slope_out).astype(jnp.bfloat16)
    grouped = hidden.reshape(rows_local, groups_local, block_width)
    pre_act = jnp.einsum(
        "rgj,gjk->rgk", grouped, channel_blocks, preferred_element_type=jnp.float32
    )
    activated = jax.nn.gelu(pre_act).astype(jnp.bfloat16)
    added = group_apply(activated, group_mix)
    outputs = (
        (grouped.astype(jnp.float32) + added).astype(jnp.bfloat16).reshape(rows_local, width_local)
    )
    upstream = cotangent.reshape(rows_local, groups_local, block_width)
    act_grad = group_apply(upstream, jnp.swapaxes(group_mix, 1, 2)).astype(jnp.bfloat16)
    pre_grad = jax.vjp(jax.nn.gelu, pre_act)[1](act_grad.astype(jnp.float32))[0].astype(
        jnp.bfloat16
    )
    back_term = jnp.einsum(
        "rgk,gjk->rgj", pre_grad, channel_blocks, preferred_element_type=jnp.float32
    )
    hidden_grad = (upstream.astype(jnp.float32) + back_term).astype(jnp.bfloat16)
    channel_grad = jnp.transpose(
        lax.psum_scatter(
            jnp.einsum("rgj,rgk->jgk", grouped, pre_grad, preferred_element_type=jnp.float32),
            "seq",
            scatter_dimension=0,
            tiled=True,
        ),
        (1, 0, 2),
    )
    grad_cube = hidden_grad.astype(jnp.float32).reshape(count_a, length_q, width_local)
    gated_grad = (grad_cube * slope_out).astype(jnp.bfloat16)
    turned_grad = to_columns(gated_grad)
    second_grad = jnp.einsum(
        "cea,ecd->acd", second_blocks, turned_grad, preferred_element_type=jnp.float32
    ).astype(jnp.bfloat16)
    first_grad = to_rows(second_grad)
    block_grad = jnp.transpose(
        lax.psum_scatter(
            jnp.einsum("acd,abd->cab", first_grad, gated, preferred_element_type=jnp.float32),
            "ch",
            scatter_dimension=0,
            tiled=True,
        ),
        (1, 0, 2),
    )
    spread = jnp.einsum(
        "acb,acd->abd", first_blocks, first_grad, preferred_element_type=jnp.float32
    )
    input_grad = grad_cube + spread * (slope_in + gate_in * source * slope_in * (1.0 - slope_in))
    input_grad = input_grad + grad_cube * returned * slope_out * (1.0 - slope_out) * gate_out
    input_grad = input_grad.astype(jnp.bfloat16).reshape(rows_local, width_local)
    return (outputs, input_grad, channel_grad, block_grad)


def solution(mesh):
    placed = (
        P("seq", "ch"),
        P("ch"),
        P("ch"),
        P("seq", None, None),
        P("seq", None, None),
        P("ch", None, None),
        P(),
        P("seq", "ch"),
    )
    return jax.shard_map(
        on_device,
        mesh=mesh,
        in_specs=placed,
        out_specs=(P("seq", "ch"), P("seq", "ch"), P("ch", "seq", None), P("seq", "ch", None)),
        check_vma=False,
    )
```

profile of v0, /device:TPU:0, one launch (start us, length us, event | category | flops | bytes accessed | tf_op | source)
XLA Modules:
  0.0 200.9 jit_solution(14426602700680347038)
XLA Ops:
  8.0 1.8 fusion.10
  9.8 0.9 copy.61
  10.7 0.5 broadcast.53
  11.2 3.8 %reduce.1 = bf16[512,512]{1,0:T(8,128)(2,1)S(1)} reduce(bf16[512,1,512]{2,1,0:T(2,128)(2,1)S(1)} %bitcast.112, bf16[]{:T(256)} %broadcast.53), dimensions={1}, to_apply=%bitcast.86.reduce_sub_computation | reduce | bytes 1048578
  15.0 1.2 reshape.163
  16.2 5.3 %all-to-all-start = ((bf16[8,2,16384]{2,1,0:T(2,128)(2,1)}), bf16[8,2,16384]{2,1,0:T(2,128)(2,1)S(1)}, u32[]{:S(2)}, u32[]{:S(2)}) async-start(bf16[8,2,16384]{2,1,0:T(2,128)(2,1)} %reshape.163), calls=%async_computation | async-start | bytes 1048576 | tf_op jit(solution)/shard_map/all_to_all | solution.py:8
  21.5 0.9 copy.70
  22.4 3.8 %reduce = bf16[512,512]{1,0:T(8,128)(2,1)S(1)} reduce(bf16[512,1,512]{2,1,0:T(2,128)(2,1)S(1)} %bitcast.115, bf16[]{:T(256)} %broadcast.53), dimensions={1}, to_apply=%bitcast.90.reduce_sub_computation | reduce | bytes 1048578
  26.2 1.2 reshape.167
  27.4 3.8 %all-to-all-done = bf16[8,2,16384]{2,1,0:T(2,128)(2,1)S(1)} async-done(((bf16[8,2,16384]{2,1,0:T(2,128)(2,1)}), bf16[8,2,16384]{2,1,0:T(2,128)(2,1)S(1)}, u32[]{:S(2)}, u32[]{:S(2)}) %all-to-all-start) | async-done | bytes 524320 | tf_op jit(solution)/shard_map/all_to_all | solution.py:8
  31.3 4.9 %all-to-all-start.4 = ((bf16[4,2,32768]{2,1,0:T(2,128)(2,1)}), bf16[4,2,32768]{2,1,0:T(2,128)(2,1)S(1)}, u32[]{:S(2)}, u32[]{:S(2)}) async-start(bf16[4,2,32768]{2,1,0:T(2,128)(2,1)} %reshape.167), calls=%async_computation.4 | async-start | bytes 1048576 | tf_op jit(solution)/shard_map/all_to_all | solution.py:21
  36.1 0.1 copy.77
  36.3 0.5 reshape.164
  36.8 0.1 copy.86
  37.0 0.4 fusion.8
  37.4 0.9 copy.64
  38.3 9.9 %all-to-all-done.4 = bf16[4,2,32768]{2,1,0:T(2,128)(2,1)S(1)} async-done(((bf16[4,2,32768]{2,1,0:T(2,128)(2,1)}), bf16[4,2,32768]{2,1,0:T(2,128)(2,1)S(1)}, u32[]{:S(2)}, u32[]{:S(2)}) %all-to-all-start.4) | async-done | bytes 524320 | tf_op jit(solution)/shard_map/all_to_all | solution.py:21
  48.3 4.4 %all-to-all-start.1 = ((bf16[8,64,512]{2,1,0:T(8,128)(2,1)}), bf16[8,64,512]{2,1,0:T(8,128)(2,1)}, u32[]{:S(2)}, u32[]{:S(2)}) async-start(bf16[8,64,512]{2,1,0:T(8,128)(2,1)} %copy.64), calls=%async_computation.1 | async-start | bytes 1048576 | tf_op jit(solution)/shard_map/all_to_all | solution.py:12
  52.7 0.7 constant_dynamic-slice_fusion
  53.4 0.2 copy.90
  53.6 0.5 reshape.168
  54.1 0.1 copy.88
  54.2 0.6 convolution_bitcast_fusion.4
  54.8 0.9 copy.73
  55.7 6.8 %all-to-all-done.1 = bf16[8,64,512]{2,1,0:T(8,128)(2,1)} async-done(((bf16[8,64,512]{2,1,0:T(8,128)(2,1)}), bf16[8,64,512]{2,1,0:T(8,128)(2,1)}, u32[]{:S(2)}, u32[]{:S(2)}) %all-to-all-start.1) | async-done | bytes 524320 | tf_op jit(solution)/shard_map/all_to_all | solution.py:12
  62.5 3.7 %all-to-all-start.5 = ((bf16[512,4,128]{0,2,1:T(8,128)(2,1)}), bf16[512,4,128]{0,2,1:T(8,128)(2,1)S(1)}, u32[]{:S(2)}, u32[]{:S(2)}) async-start(bf16[512,4,128]{0,2,1:T(8,128)(2,1)} %copy.73), calls=%async_computation.5 | async-start | bytes 1048576 | tf_op jit(solution)/shard_map/all_to_all | solution.py:25
  66.2 1.4 fusion.32
  67.6 10.8 %all-to-all-done.5 = bf16[512,4,128]{0,2,1:T(8,128)(2,1)S(1)} async-done(((bf16[512,4,128]{0,2,1:T(8,128)(2,1)}), bf16[512,4,128]{0,2,1:T(8,128)(2,1)S(1)}, u32[]{:S(2)}, u32[]{:S(2)}) %all-to-all-start.5) | async-done | bytes 524320 | tf_op jit(solution)/shard_map/all_to_all | solution.py:25
  78.5 1.3 copy.85
  79.9 3.1 %fusion.22 = (bf16[512,1,512]{2,0,1:T(8,128)(2,1)S(1)}, bf16[512,1,512]{2,0,1:T(8,128)(2,1)}) fusion(f32[512,1,512]{2,0,1:T(8,128)} %copy.85, bf16[512,512]{1,0:T(8,128)(2,1)S(1)} %fusion.32, bf16[1,512,512]{2,1,0:T(8,128)(2,1)S(1)} %copy-done), kind=kOutput, calls=%fused_computation.42 | convolution fusion | flops 274202624 | bytes 3145728 | tf_op jit(solution)/shard_map/rgj,gjk->rgk/dot_general | solution.py:51
  82.9 0.5 fusion.7
  83.4 0.3 copy-done.7
  83.7 0.8 copy-done.5
  84.6 0.3 fusion.33
  84.9 0.8 copy.100
  85.7 3.8 %reduce.3 = bf16[512,512]{1,0:T(8,128)(2,1)S(1)} reduce(bf16[512,1,512]{2,1,0:T(2,128)(2,1)S(1)} %bitcast.114, bf16[]{:T(256)} %broadcast.53), dimensions={1}, to_apply=%bitcast.105.reduce_sub_computation | reduce | bytes 1048578
  89.5 1.2 reshape.169
  90.7 4.5 %all-to-all-start.6 = ((bf16[8,2,16384]{2,1,0:T(2,128)(2,1)}), bf16[8,2,16384]{2,1,0:T(2,128)(2,1)S(1)}, u32[]{:S(2)}, u32[]{:S(2)}) async-start(bf16[8,2,16384]{2,1,0:T(2,128)(2,1)} %reshape.169), calls=%async_computation.6 | async-start | bytes 1048576 | tf_op jit(solution)/shard_map/all_to_all | solution.py:8
  95.3 0.9 copy.66
  96.2 3.8 %reduce.2 = bf16[512,512]{1,0:T(8,128)(2,1)S(1)} reduce(bf16[512,1,512]{2,1,0:T(2,128)(2,1)S(1)} %bitcast.113, bf16[]{:T(256)} %broadcast.53), dimensions={1}, to_apply=%bitcast.88.reduce_sub_computation | reduce | bytes 1048578
  100.0 1.2 reshape.165
  101.2 3.8 %all-to-all-done.6 = bf16[8,2,16384]{2,1,0:T(2,128)(2,1)S(1)} async-done(((bf16[8,2,16384]{2,1,0:T(2,128)(2,1)}), bf16[8,2,16384]{2,1,0:T(2,128)(2,1)S(1)}, u32[]{:S(2)}, u32[]{:S(2)}) %all-to-all-start.6) | async-done | bytes 524320 | tf_op jit(solution)/shard_map/all_to_all | solution.py:8
  105.0 3.5 %all-to-all-start.2 = ((bf16[4,2,32768]{2,1,0:T(2,128)(2,1)}), bf16[4,2,32768]{2,1,0:T(2,128)(2,1)S(1)}, u32[]{:S(2)}, u32[]{:S(2)}) async-start(bf16[4,2,32768]{2,1,0:T(2,128)(2,1)} %reshape.165), calls=%async_computation.2 | async-start | bytes 1048576 | tf_op jit(solution)/shard_map/all_to_all | solution.py:21
  108.5 0.5 reshape.170
  109.2 0.4 fusion.9
  109.6 0.9 copy.78
  110.5 10.3 %all-to-all-done.2 = bf16[4,2,32768]{2,1,0:T(2,128)(2,1)S(1)} async-done(((bf16[4,2,32768]{2,1,0:T(2,128)(2,1)}), bf16[4,2,32768]{2,1,0:T(2,128)(2,1)S(1)}, u32[]{:S(2)}, u32[]{:S(2)}) %all-to-all-start.2) | async-done | bytes 524320 | tf_op jit(solution)/shard_map/all_to_all | solution.py:21
  120.9 4.4 %all-to-all-start.7 = ((bf16[8,64,512]{2,1,0:T(8,128)(2,1)}), bf16[8,64,512]{2,1,0:T(8,128)(2,1)}, u32[]{:S(2)}, u32[]{:S(2)}) async-start(bf16[8,64,512]{2,1,0:T(8,128)(2,1)} %copy.78), calls=%async_computation.7 | async-start | bytes 1048576 | tf_op jit(solution)/shard_map/all_to_all | solution.py:12
  125.3 0.5 convolution_bitcast_fusion.1
  125.8 1.9 copy.80
  127.8 0.5 reshape.166
  128.5 6.6 %all-to-all-done.7 = bf16[8,64,512]{2,1,0:T(8,128)(2,1)} async-done(((bf16[8,64,512]{2,1,0:T(8,128)(2,1)}), bf16[8,64,512]{2,1,0:T(8,128)(2,1)}, u32[]{:S(2)}, u32[]{:S(2)}) %all-to-all-start.7) | async-done | bytes 524320 | tf_op jit(solution)/shard_map/all_to_all | solution.py:12
  135.1 2.5 %convolution_bitcast_fusion = f32[512,1,512]{0,2,1:T(8,128)} fusion(bf16[512,512]{1,0:T(8,128)(2,1)} %bitcast.25, bf16[512,512]{1,0:T(8,128)(2,1)S(1)} %copy-done.4, f32[512]{0:T(512)S(1)} %copy-done.12), kind=kOutput, calls=%fused_computation.9 | convolution fusion | flops 270270464 | bytes 2099200 | tf_op jit(solution)/shard_map/acd,abd->cab/dot_general | solution.py:86
  137.7 0.5 convolution_bitcast_fusion.5
  138.2 1.3 copy.68
  139.5 3.7 %all-to-all-start.3 = ((f32[512,4,128]{0,2,1:T(8,128)}), f32[512,4,128]{0,2,1:T(8,128)S(1)}, u32[]{:S(2)}, u32[]{:S(2)}) async-start(f32[512,4,128]{0,2,1:T(8,128)} %copy.68), calls=%async_computation.3 | async-start | bytes 2097152 | tf_op jit(solution)/shard_map/all_to_all | solution.py:25
  143.2 0.6 dynamic-slice.1
  144.4 41.0 %all-reduce.3.cloned.1.call-done = f32[512,1,512]{2,1,0:T(1,128)} async-done(((f32[512,1,512]{2,1,0:T(1,128)}), f32[512,1,512]{2,1,0:T(1,128)}) %all-reduce.3.cloned.1.call-update) | async-done | bytes 1048592
  185.4 0.9 dynamic-slice_bitcast_fusion
  186.3 0.7 copy.81
  187.0 3.3 %fusion.4 = bf16[512,512]{1,0:T(8,128)(2,1)} fusion(bf16[512,512]{1,0:T(8,128)(2,1)} %bitcast.25, bf16[512,512]{1,0:T(8,128)(2,1)S(1)} %copy-done.6, bf16[512,512]{1,0:T(8,128)(2,1)S(1)} %copy-done.4, bf16[512,512]{1,0:T(8,128)(2,1)} %bitcast.27, bf16[1,512,512]{2,1,0:T(8,128)(2,1)} %param.11, f32[512]{0:T(512)S(1)} %copy-done.11, f32[512]{0:T(512)S(1)} %copy-done.12), kind=kOutput, calls=%fused_computation.24 | convolution fusion | flops 274726912 | bytes 3149824 | tf_op jit(solution)/shard_map/acb,acd->abd/dot_general | solution.py:93
  190.3 0.3 copy.69
  190.7 1.0 add_convert_fusion
  191.6 1.8 copy.82
  (35 shorter events, 0.5 us)
Async XLA Ops:
  8.0 71.9 %copy-start = (bf16[1,512,512]{2,1,0:T(8,128)(2,1)S(1)}, bf16[1,512,512]{2,1,0:T(8,128)(2,1)}, u32[]{:S(2)}) copy-start(bf16[1,512,512]{2,1,0:T(8,128)(2,1)} %param.13) | copy-start | bytes 1572868
  16.2 5.3 %copy-start.1 = (bf16[512,512]{1,0:T(8,128)(2,1)S(1)}, bf16[512,512]{1,0:T(8,128)(2,1)}, u32[]{:S(2)}) copy-start(bf16[512,512]{1,0:T(8,128)(2,1)} %param.15) | copy-start | bytes 1572868
  16.2 15.0 %all-to-all-start = ((bf16[8,2,16384]{2,1,0:T(2,128)(2,1)}), bf16[8,2,16384]{2,1,0:T(2,128)(2,1)S(1)}, u32[]{:S(2)}, u32[]{:S(2)}) async-start(bf16[8,2,16384]{2,1,0:T(2,128)(2,1)} %reshape.163), calls=%async_computation | async-start | bytes 1048576 | tf_op jit(solution)/shard_map/all_to_all | solution.py:8
  27.4 8.7 %copy-start.10 = (bf16[64,8,8]{0,2,1:T(8,128)(2,1)S(1)}, bf16[64,8,8]{0,2,1:T(8,128)(2,1)}, u32[]{:S(2)}) copy-start(bf16[64,8,8]{0,2,1:T(8,128)(2,1)} %param.12) | copy-start | bytes 24580
  31.3 17.0 %all-to-all-start.4 = ((bf16[4,2,32768]{2,1,0:T(2,128)(2,1)}), bf16[4,2,32768]{2,1,0:T(2,128)(2,1)S(1)}, u32[]{:S(2)}, u32[]{:S(2)}) async-start(bf16[4,2,32768]{2,1,0:T(2,128)(2,1)} %reshape.167), calls=%async_computation.4 | async-start | bytes 1048576 | tf_op jit(solution)/shard_map/all_to_all | solution.py:21
  48.3 14.3 %all-to-all-start.1 = ((bf16[8,64,512]{2,1,0:T(8,128)(2,1)}), bf16[8,64,512]{2,1,0:T(8,128)(2,1)}, u32[]{:S(2)}, u32[]{:S(2)}) async-start(bf16[8,64,512]{2,1,0:T(8,128)(2,1)} %copy.64), calls=%async_computation.1 | async-start | bytes 1048576 | tf_op jit(solution)/shard_map/all_to_all | solution.py:12
  55.7 10.5 %copy-start.2 = (bf16[512,512]{1,0:T(8,128)(2,1)S(1)}, bf16[512,512]{1,0:T(8,128)(2,1)}, u32[]{:S(2)}) copy-start(bf16[512,512]{1,0:T(8,128)(2,1)} %param.8) | copy-start | bytes 1572868
  55.7 10.5 %copy-start.11 = (f32[512]{0:T(512)S(1)}, f32[512]{0:T(512)}, u32[]{:S(2)}) copy-start(f32[512]{0:T(512)} %param.10) | copy-start | bytes 6148
  62.5 15.9 %all-to-all-start.5 = ((bf16[512,4,128]{0,2,1:T(8,128)(2,1)}), bf16[512,4,128]{0,2,1:T(8,128)(2,1)S(1)}, u32[]{:S(2)}, u32[]{:S(2)}) async-start(bf16[512,4,128]{0,2,1:T(8,128)(2,1)} %copy.73), calls=%async_computation.5 | async-start | bytes 1048576 | tf_op jit(solution)/shard_map/all_to_all | solution.py:25
  82.9 0.8 copy-start.7
  82.9 1.6 copy-start.3
  83.7 0.8 copy-start.5
  90.7 4.6 %copy-start.9 = (bf16[512,1,512]{2,0,1:T(8,128)(2,1)S(1)}, bf16[512,1,512]{2,0,1:T(8,128)(2,1)}, u32[]{:S(2)}) copy-start(bf16[512,1,512]{2,0,1:T(8,128)(2,1)} %get-tuple-element.21) | copy-start | bytes 1572868
  90.7 14.3 %all-to-all-start.6 = ((bf16[8,2,16384]{2,1,0:T(2,128)(2,1)}), bf16[8,2,16384]{2,1,0:T(2,128)(2,1)S(1)}, u32[]{:S(2)}, u32[]{:S(2)}) async-start(bf16[8,2,16384]{2,1,0:T(2,128)(2,1)} %reshape.169), calls=%async_computation.6 | async-start | bytes 1048576 | tf_op jit(solution)/shard_map/all_to_all | solution.py:8
  105.0 15.9 %all-to-all-start.2 = ((bf16[4,2,32768]{2,1,0:T(2,128)(2,1)}), bf16[4,2,32768]{2,1,0:T(2,128)(2,1)S(1)}, u32[]{:S(2)}, u32[]{:S(2)}) async-start(bf16[4,2,32768]{2,1,0:T(2,128)(2,1)} %reshape.165), calls=%async_computation.2 | async-start | bytes 1048576 | tf_op jit(solution)/shard_map/all_to_all | solution.py:21
  110.5 14.8 %copy-start.8 = (bf16[512,1,512]{2,0,1:T(8,128)(2,1)S(1)}, bf16[512,1,512]{2,0,1:T(8,128)(2,1)}, u32[]{:S(2)}) copy-start(bf16[512,1,512]{2,0,1:T(8,128)(2,1)} %copy-done.7) | copy-start | bytes 1572868
  120.9 14.3 %all-to-all-start.7 = ((bf16[8,64,512]{2,1,0:T(8,128)(2,1)}), bf16[8,64,512]{2,1,0:T(8,128)(2,1)}, u32[]{:S(2)}, u32[]{:S(2)}) async-start(bf16[8,64,512]{2,1,0:T(8,128)(2,1)} %copy.78), calls=%async_computation.7 | async-start | bytes 1048576 | tf_op jit(solution)/shard_map/all_to_all | solution.py:12
  125.3 60.1 %all-reduce.3.cloned.1.call-start = ((), (), s32[]{:S(2)}) async-start(), calls=%async_computation.10 | async-start | bytes 2097152
  127.8 63.9 %reduce-scatter.2.cloned.1.call-start = ((), (), s32[]{:S(2)}) async-start(), calls=%async_computation.9 | async-start | bytes 1310720 | tf_op jit(solution)/shard_map/reduce_scatter | solution.py:85
  128.4 6.8 %copy-start.4 = (bf16[512,512]{1,0:T(8,128)(2,1)S(1)}, bf16[512,512]{1,0:T(8,128)(2,1)}, u32[]{:S(2)}) copy-start(bf16[512,512]{1,0:T(8,128)(2,1)} %param.8) | copy-start | bytes 1572868
  128.4 6.8 %copy-start.12 = (f32[512]{0:T(512)S(1)}, f32[512]{0:T(512)}, u32[]{:S(2)}) copy-start(f32[512]{0:T(512)} %param.9) | copy-start | bytes 6148
  139.5 3.7 %copy-start.13 = (u32[32]{0:T(128)S(1)}, u32[32]{0:T(128)}, u32[]{:S(2)}) copy-start(u32[32]{0:T(128)} %constant.27) | copy-start | bytes 388
  139.5 50.9 %all-to-all-start.3 = ((f32[512,4,128]{0,2,1:T(8,128)}), f32[512,4,128]{0,2,1:T(8,128)S(1)}, u32[]{:S(2)}, u32[]{:S(2)}) async-start(f32[512,4,128]{0,2,1:T(8,128)} %copy.68), calls=%async_computation.3 | async-start | bytes 2097152 | tf_op jit(solution)/shard_map/all_to_all | solution.py:25
  143.1 43.9 %copy-start.6 = (bf16[512,512]{1,0:T(8,128)(2,1)S(1)}, bf16[512,512]{1,0:T(8,128)(2,1)}, u32[]{:S(2)}) copy-start(bf16[512,512]{1,0:T(8,128)(2,1)} %copy-done.5) | copy-start | bytes 1572868
Sparse Core Ops, SparseCore 0:
  129.3 56.0 all-reduce.2
Sparse Core Ops, SparseCore 1:
  137.8 39.2 reduce-scatter.1
where the time goes:
time: 202 us; the launch traced here: 201 us
  waiting for transfers between devices  93.2 us (46%)
  starting transfers between devices  34.4 us (17%)
  local copies, waits for them, and re-layouts  25.2 us (12%)
  other arithmetic  18.1 us (9%)
  between operations  16.5 us (8%)
  matrix products  13.6 us (7%)
    unnamed x3, waiting for transfers between devices  41 us
    all_to_all x2, waiting for transfers between devices, group_apply(): lax.all_to_all(blocks, 'ch', split_axis=2, concat_axis=1, tiled=True)  20.3 us
    unnamed x4, other arithmetic  15.3 us
    all_to_all x2, waiting for transfers between devices, to_rows(): lax.all_to_all(values, 'seq', split_axis=0, concat_axis=1, tiled=True)  13.4 us
    unnamed x46, local copies, waits for them, and re-layouts  12.4 us
    all_to_all x2, waiting for transfers between devices, group_apply(): return lax.all_to_all(mixed, 'ch', split_axis=1, concat_axis=2, tiled=True)  10.8 us
    all_to_all x2, starting transfers between devices, to_columns(): lax.all_to_all(values, 'seq', split_axis=1, concat_axis=0, tiled=True)  9.85 us
    all_to_all x2, starting transfers between devices, to_rows(): lax.all_to_all(values, 'seq', split_axis=0, concat_axis=1, tiled=True)  8.83 us
  transfers between devices with their start and end apart: 10, of which 8 were waited for; matrix products, arithmetic and copies ran while one was open for 17% of the time, Pallas kernels for 0%

commit v1 on v0

--- a/solution.py
+++ b/solution.py
@@ -5,24 +5,18 @@
 
 
 def to_columns(values):
-    return lax.all_to_all(values, "seq", split_axis=1, concat_axis=0, tiled=True)
+    n = lax.axis_size("seq")
+    pieces = values.reshape(n, values.shape[1] // n, values.shape[2])
+    return lax.all_to_all(pieces, "seq", split_axis=0, concat_axis=0, tiled=True)
 
 
 def to_rows(values):
-    return lax.all_to_all(values, "seq", split_axis=0, concat_axis=1, tiled=True)
+    back = lax.all_to_all(values, "seq", split_axis=0, concat_axis=0, tiled=True)
+    return back.reshape(back.shape[0] * back.shape[1], back.shape[2])
 
 
-def group_apply(blocks, table):
-    owner = lax.axis_index("ch")
-    narrow = blocks.shape[2] // lax.axis_size("ch")
-    table_rows = lax.dynamic_slice_in_dim(table, owner * narrow, narrow, 0)
-    mixed = jnp.einsum(
-        "rgk,kgh->rhk",
-        lax.all_to_all(blocks, "ch", split_axis=2, concat_axis=1, tiled=True),
-        table_rows,
-        preferred_element_type=jnp.float32,
-    )
-    return lax.all_to_all(mixed, "ch", split_axis=1, concat_axis=2, tiled=True)
+def gather_groups(blocks):
+    return lax.all_gather(blocks, "ch", axis=0, tiled=False)
 
 
 def on_device(
@@ -34,6 +28,16 @@
     width_local = inputs.shape[1]
     groups_local = channel_blocks.shape[0]
     block_width = channel_blocks.shape[1]
+    me = lax.axis_index("ch")
+    mix_f = group_mix.astype(jnp.float32)
+    mix_out = lax.dynamic_index_in_dim(mix_f, me, axis=2, keepdims=False)
+    mix_back = lax.dynamic_index_in_dim(mix_f, me, axis=1, keepdims=False)
+
+    upstream = cotangent.reshape(rows_local, groups_local, block_width)
+    every_upstream = gather_groups(cotangent).astype(jnp.float32)
+    act_grad = jnp.einsum("hrk,kh->rk", every_upstream, mix_back).astype(jnp.bfloat16)
+    act_grad = act_grad.reshape(rows_local, groups_local, block_width)
+
     source = inputs.astype(jnp.float32).reshape(count_a, length_q, width_local)
     slope_in = jax.nn.sigmoid(gate_in * source)
     gated = (source * slope_in).astype(jnp.bfloat16)
@@ -44,7 +48,7 @@
     mixed_second = jnp.einsum(
         "cea,acd->ecd", second_blocks, turned, preferred_element_type=jnp.float32
     ).astype(jnp.bfloat16)
-    returned = to_rows(mixed_second).astype(jnp.float32)
+    returned = to_rows(mixed_second).astype(jnp.float32).reshape(count_a, length_q, width_local)
     slope_out = jax.nn.sigmoid(gate_out * source)
     hidden = (source + returned * slope_out).astype(jnp.bfloat16)
     grouped = hidden.reshape(rows_local, groups_local, block_width)
@@ -52,12 +56,12 @@
         "rgj,gjk->rgk", grouped, channel_blocks, preferred_element_type=jnp.float32
     )
     activated = jax.nn.gelu(pre_act).astype(jnp.bfloat16)
-    added = group_apply(activated, group_mix)
+    every_activated = gather_groups(activated.reshape(rows_local, block_width))
+    added = jnp.einsum("grk,kg->rk", every_activated.astype(jnp.float32), mix_out)
     outputs = (
-        (grouped.astype(jnp.float32) + added).astype(jnp.bfloat16).reshape(rows_local, width_local)
+        (grouped.astype(jnp.float32).reshape(rows_local, width_local) + added)
+        .astype(jnp.bfloat16)
     )
-    upstream = cotangent.reshape(rows_local, groups_local, block_width)
-    act_grad = group_apply(upstream, jnp.swapaxes(group_mix, 1, 2)).astype(jnp.bfloat16)
     pre_grad = jax.vjp(jax.nn.gelu, pre_act)[1](act_grad.astype(jnp.float32))[0].astype(
         jnp.bfloat16
     )
@@ -80,7 +84,7 @@
     second_grad = jnp.einsum(
         "cea,ecd->acd", second_blocks, turned_grad, preferred_element_type=jnp.float32
     ).astype(jnp.bfloat16)
-    first_grad = to_rows(second_grad)
+    first_grad = to_rows(second_grad).reshape(count_a, length_q, width_local)
     block_grad = jnp.transpose(
         lax.psum_scatter(
             jnp.einsum("acd,abd->cab", first_grad, gated, preferred_element_type=jnp.float32),

time: 202 us -> 228 us (1.13)
  waiting for transfers between devices: 93.2 us -> 159 us
  starting transfers between devices: 34.4 us -> 13.1 us
  local copies, waits for them, and re-layouts: 25.2 us -> 7.99 us
  blocking collectives: 0 us -> 13.2 us
  other arithmetic: 18.1 us -> 5.54 us
    all_gather x0 -> x2, waiting for transfers between devices: none -> 62.7 us  [gather_groups(): return lax.all_gather(blocks, 'ch', axis=0, tiled=False)]
    all_to_all x8 -> x3, waiting for transfers between devices: 52.1 us -> 25.4 us  [the longest x2 15.8 us: to_rows(): lax.all_to_all(values, 'seq', split_axis=0, concat_axis=0, tiled=True)]
    reduce_scatter x1, waiting for transfers between devices: 0.01 us -> 23.9 us  [on_device(): lax.psum_scatter(jnp.einsum('acd,abd->cab', first_grad, gated, preferred_...]
    all_to_all x8 -> x3, starting transfers between devices: 34.3 us -> 12.9 us  [the longest x2 7.64 us: to_rows(): lax.all_to_all(values, 'seq', split_axis=0, concat_axis=0, tiled=True)]
    unnamed x4 -> x2, other arithmetic: 15.3 us -> 0.02 us
    all_to_all x0 -> x1, blocking collectives: none -> 13.2 us  [to_columns(): lax.all_to_all(pieces, 'seq', split_axis=0, concat_axis=0, tiled=True)]
    unnamed x46 -> x26, local copies, waits for them, and re-layouts: 12.4 us -> 3.23 us
    unnamed x3 -> x5, waiting for transfers between devices: 41 us -> 46.9 us
  transfers between devices with their start and end apart: 10 -> 7, of which waited for: 8 -> 7; matrix products, arithmetic and copies ran while one was open for 17% -> 8% of each run, Pallas kernels for 0% -> 0%
where the time goes in v1:
time: 228 us; the launch traced here: 227 us
  waiting for transfers between devices  159 us (70%)
  between operations  14.6 us (6%)
  matrix products  13.8 us (6%)
  blocking collectives  13.2 us (6%)
  starting transfers between devices  13.1 us (6%)
  local copies, waits for them, and re-layouts  7.99 us (4%)
  other arithmetic  5.54 us (2%)
    all_gather x2, waiting for transfers between devices, gather_groups(): return lax.all_gather(blocks, 'ch', axis=0, tiled=False)  62.7 us
    unnamed x5, waiting for transfers between devices  46.9 us
    reduce_scatter x1, waiting for transfers between devices, on_device(): lax.psum_scatter(jnp.einsum('acd,abd->cab', first_grad, gated, preferred_...  23.9 us
    all_to_all x2, waiting for transfers between devices, to_rows(): lax.all_to_all(values, 'seq', split_axis=0, concat_axis=0, tiled=True)  15.8 us
    all_to_all x1, blocking collectives, to_columns(): lax.all_to_all(pieces, 'seq', split_axis=0, concat_axis=0, tiled=True)  13.2 us
    all_to_all x1, waiting for transfers between devices, to_columns(): lax.all_to_all(pieces, 'seq', split_axis=0, concat_axis=0, tiled=True)  9.59 us
    all_to_all x2, starting transfers between devices, to_rows(): lax.all_to_all(values, 'seq', split_axis=0, concat_axis=0, tiled=True)  7.64 us
    all_to_all x1, starting transfers between devices, to_columns(): lax.all_to_all(pieces, 'seq', split_axis=0, concat_axis=0, tiled=True)  5.31 us
  transfers between devices with their start and end apart: 7, of which 7 were waited for; matrix products, arithmetic and copies ran while one was open for 8% of the time, Pallas kernels for 0%

profile of v1, /device:TPU:0, one launch (start us, length us, event | category | flops | bytes accessed | tf_op | source)
XLA Modules:
  0.0 227.0 jit_solution(12649347416051719349)
XLA Ops:
  7.2 0.0 copy-start
  7.2 0.0 all-gather.7.cloned.1.call-start
  7.2 0.7 all-gather.7.cloned.1.call-update
  7.9 0.0 copy-start.4
  7.9 2.6 %convolution_convert_fusion = bf16[512,512]{0,1:T(8,128)(2,1)} fusion(bf16[1,512,512]{2,1,0:T(8,128)(2,1)} %param.11, bf16[512,512]{1,0:T(8,128)(2,1)} %param.8, f32[512]{0:T(512)} %param.9), kind=kOutput, calls=%fused_computation.20 | convolution fusion | flops 270532608 | bytes 1574912 | tf_op jit(solution)/shard_map/acb,abd->acd/dot_general | solution.py:44
  10.5 0.0 copy-start.5
  10.5 0.0 copy-start.2
  10.5 0.0 copy-start.6
  10.5 5.3 %all-to-all-start = ((bf16[8,64,512]{2,1,0:T(8,128)(2,1)}), bf16[8,64,512]{2,1,0:T(8,128)(2,1)S(1)}, u32[]{:S(2)}, u32[]{:S(2)}) async-start(bf16[8,64,512]{2,1,0:T(8,128)(2,1)} %bitcast.4), calls=%async_computation | async-start | bytes 1048576 | tf_op jit(solution)/shard_map/all_to_all | solution.py:10
  15.8 0.0 copy-done.4
  15.8 0.1 copy.32
  15.9 9.6 %all-to-all-done = bf16[8,64,512]{2,1,0:T(8,128)(2,1)S(1)} async-done(((bf16[8,64,512]{2,1,0:T(8,128)(2,1)}), bf16[8,64,512]{2,1,0:T(8,128)(2,1)S(1)}, u32[]{:S(2)}, u32[]{:S(2)}) %all-to-all-start) | async-done | bytes 524320 | tf_op jit(solution)/shard_map/all_to_all | solution.py:10
  25.5 0.4 fusion.8
  26.0 0.9 copy.30
  26.9 3.5 %all-to-all-start.1 = ((bf16[8,64,512]{2,1,0:T(8,128)(2,1)}), bf16[8,64,512]{2,1,0:T(8,128)(2,1)S(1)}, u32[]{:S(2)}, u32[]{:S(2)}) async-start(bf16[8,64,512]{2,1,0:T(8,128)(2,1)} %copy.30), calls=%async_computation.1 | async-start | bytes 1048576 | tf_op jit(solution)/shard_map/all_to_all | solution.py:14
  30.4 0.0 copy-done.5
  30.5 9.6 %all-to-all-done.1 = bf16[8,64,512]{2,1,0:T(8,128)(2,1)S(1)} async-done(((bf16[8,64,512]{2,1,0:T(8,128)(2,1)}), bf16[8,64,512]{2,1,0:T(8,128)(2,1)S(1)}, u32[]{:S(2)}, u32[]{:S(2)}) %all-to-all-start.1) | async-done | bytes 524320 | tf_op jit(solution)/shard_map/all_to_all | solution.py:14
  40.1 0.0 copy-done.2
  40.1 0.0 copy-done.6
  40.1 0.4 fusion.31
  40.5 17.8 %all-gather.7.cloned.1.call-done = bf16[2048,512]{1,0:T(8,128)(2,1)} async-done(((bf16[512,512]{1,0:T(8,128)(2,1)}), bf16[2048,512]{1,0:T(8,128)(2,1)}) %all-gather.7.cloned.1.call-update) | async-done | bytes 2097168 | tf_op jit(solution)/shard_map/all_gather | solution.py:19
  58.3 2.0 multiply_reduce_fusion
  60.3 0.0 copy-done
  60.3 0.0 copy-start.1
  60.3 1.9 fusion.21
  62.2 0.0 copy-start.3
  62.2 0.0 copy-done.1
  62.2 1.4 fusion.22
  63.6 0.0 copy-done.3
  63.6 13.2 %all_to_all.20 = bf16[8,64,512]{2,1,0:T(8,128)(2,1)S(1)} all-to-all(bf16[8,64,512]{2,1,0:T(8,128)(2,1)S(1)} %bitcast.118), channel_id=1, replica_groups=mesh['seq'=8,'ch'=4] {'seq'}, dimensions={0} | all-to-all | bytes 1048576 | tf_op jit(solution)/shard_map/all_to_all | solution.py:10
  76.8 0.4 fusion.9
  77.2 0.9 copy.33
  78.2 4.1 %all-to-all-start.3 = ((bf16[8,64,512]{2,1,0:T(8,128)(2,1)}), bf16[8,64,512]{2,1,0:T(8,128)(2,1)}, u32[]{:S(2)}, u32[]{:S(2)}) async-start(bf16[8,64,512]{2,1,0:T(8,128)(2,1)} %copy.33), calls=%async_computation.3 | async-start | bytes 1048576 | tf_op jit(solution)/shard_map/all_to_all | solution.py:14
  82.3 0.0 all-reduce.3.cloned.1.call-start
  82.4 1.5 convolution_bitcast_fusion.1
  83.9 0.0 copy-start.8
  83.9 1.9 copy.35
  85.8 0.0 all-reduce.3.cloned.1.call-update
  85.9 0.0 reduce-scatter.2.cloned.1.call-start
  85.9 6.2 %all-to-all-done.3 = bf16[8,64,512]{2,1,0:T(8,128)(2,1)} async-done(((bf16[8,64,512]{2,1,0:T(8,128)(2,1)}), bf16[8,64,512]{2,1,0:T(8,128)(2,1)}, u32[]{:S(2)}, u32[]{:S(2)}) %all-to-all-start.3) | async-done | bytes 524320 | tf_op jit(solution)/shard_map/all_to_all | solution.py:14
  92.1 0.0 copy-done.8
  92.1 0.0 copy-start.9
  92.1 2.5 %convolution_bitcast_fusion = f32[512,1,512]{0,2,1:T(8,128)} fusion(bf16[512,512]{1,0:T(8,128)(2,1)} %bitcast.31, bf16[512,512]{1,0:T(8,128)(2,1)S(1)} %copy-done.2, f32[512]{0:T(512)S(1)} %copy-done.8), kind=kOutput, calls=%fused_computation.11 | convolution fusion | flops 270270464 | bytes 2099200 | tf_op jit(solution)/shard_map/acd,abd->cab/dot_general | solution.py:90
  94.6 0.0 copy-start.7
  94.6 0.0 copy-start.10
  94.6 0.0 reduce-scatter.2.cloned.1.call-update
  94.6 0.0 all-gather.5.cloned.1.call-start
  94.7 0.5 all-gather.5.cloned.1.call-update
  95.2 0.0 copy-done.9
  95.2 0.6 dynamic-slice
  96.5 45.6 %all-reduce.3.cloned.1.call-done = f32[512,1,512]{2,1,0:T(1,128)} async-done(((f32[512,1,512]{2,1,0:T(1,128)}), f32[512,1,512]{2,1,0:T(1,128)}) %all-reduce.3.cloned.1.call-update) | async-done | bytes 1048592
  142.1 0.9 dynamic-slice_bitcast_fusion
  143.0 0.7 copy.36
  143.7 0.0 copy-done.7
  143.7 0.0 copy-done.10
  143.7 3.0 %fusion.4 = bf16[512,512]{1,0:T(8,128)(2,1)} fusion(bf16[512,512]{1,0:T(8,128)(2,1)} %bitcast.31, bf16[512,512]{1,0:T(8,128)(2,1)S(1)} %copy-done.10, bf16[512,512]{1,0:T(8,128)(2,1)S(1)} %copy-done.2, bf16[512,512]{1,0:T(8,128)(2,1)S(1)} %bitcast.117, bf16[1,512,512]{2,1,0:T(8,128)(2,1)S(1)} %copy-done.7, f32[512]{0:T(512)S(1)} %copy-done.6, ...), kind=kOutput, calls=%fused_computation.24 | convolution fusion | flops 274726912 | bytes 3149824 | tf_op jit(solution)/shard_map/acb,acd->abd/dot_general | solution.py:97
  146.7 23.9 %reduce-scatter.2.cloned.1.call-done = f32[128,1,512]{0,2,1:T(8,128)} async-done(((f32[512,1,512]{0,2,1:T(8,128)}), f32[128,1,512]{0,2,1:T(8,128)}) %reduce-scatter.2.cloned.1.call-update) | async-done | bytes 262160 | tf_op jit(solution)/shard_map/reduce_scatter | solution.py:89
  170.6 1.8 copy.37
  172.4 44.9 %all-gather.5.cloned.1.call-done = bf16[2048,1,512]{2,0,1:T(8,128)(2,1)} async-done(((bf16[512,1,512]{2,0,1:T(8,128)(2,1)}), bf16[2048,1,512]{2,0,1:T(8,128)(2,1)}) %all-gather.5.cloned.1.call-update) | async-done | bytes 2097168 | tf_op jit(solution)/shard_map/all_gather | solution.py:19
  217.4 2.2 multiply_reduce_fusion.1
  219.5 1.0 fusion.35
  (3 shorter events, 0.0 us)
Async XLA Ops:
  7.2 53.1 %copy-start = (bf16[1,512,512]{2,1,0:T(8,128)(2,1)S(1)}, bf16[1,512,512]{2,1,0:T(8,128)(2,1)}, u32[]{:S(2)}) copy-start(bf16[1,512,512]{2,1,0:T(8,128)(2,1)} %param.13) | copy-start | bytes 1572868
  7.2 51.1 %all-gather.7.cloned.1.call-start = ((), (), s32[]{:S(2)}) async-start(), calls=%async_computation.7 | async-start | bytes 2621440 | tf_op jit(solution)/shard_map/all_gather | solution.py:19
  7.9 7.9 %copy-start.4 = (bf16[64,8,8]{0,2,1:T(8,128)(2,1)S(1)}, bf16[64,8,8]{0,2,1:T(8,128)(2,1)}, u32[]{:S(2)}) copy-start(bf16[64,8,8]{0,2,1:T(8,128)(2,1)} %param.12) | copy-start | bytes 24580
  10.5 20.0 %copy-start.5 = (bf16[512,4,4]{0,2,1:T(4,128)(2,1)S(1)}, bf16[512,4,4]{0,2,1:T(4,128)(2,1)}, u32[]{:S(2)}) copy-start(bf16[512,4,4]{0,2,1:T(4,128)(2,1)} %param.14) | copy-start | bytes 49156
  10.5 29.6 %copy-start.2 = (bf16[512,512]{1,0:T(8,128)(2,1)S(1)}, bf16[512,512]{1,0:T(8,128)(2,1)}, u32[]{:S(2)}) copy-start(bf16[512,512]{1,0:T(8,128)(2,1)} %param.8) | copy-start | bytes 1572868
  10.5 29.6 %copy-start.6 = (f32[512]{0:T(512)S(1)}, f32[512]{0:T(512)}, u32[]{:S(2)}) copy-start(f32[512]{0:T(512)} %param.10) | copy-start | bytes 6148
  10.5 15.1 %all-to-all-start = ((bf16[8,64,512]{2,1,0:T(8,128)(2,1)}), bf16[8,64,512]{2,1,0:T(8,128)(2,1)S(1)}, u32[]{:S(2)}, u32[]{:S(2)}) async-start(bf16[8,64,512]{2,1,0:T(8,128)(2,1)} %bitcast.4), calls=%async_computation | async-start | bytes 1048576 | tf_op jit(solution)/shard_map/all_to_all | solution.py:10
  26.9 13.2 %all-to-all-start.1 = ((bf16[8,64,512]{2,1,0:T(8,128)(2,1)}), bf16[8,64,512]{2,1,0:T(8,128)(2,1)S(1)}, u32[]{:S(2)}, u32[]{:S(2)}) async-start(bf16[8,64,512]{2,1,0:T(8,128)(2,1)} %copy.30), calls=%async_computation.1 | async-start | bytes 1048576 | tf_op jit(solution)/shard_map/all_to_all | solution.py:14
  60.3 1.9 copy-start.1
  62.2 1.4 copy-start.3
  78.2 13.9 %all-to-all-start.3 = ((bf16[8,64,512]{2,1,0:T(8,128)(2,1)}), bf16[8,64,512]{2,1,0:T(8,128)(2,1)}, u32[]{:S(2)}, u32[]{:S(2)}) async-start(bf16[8,64,512]{2,1,0:T(8,128)(2,1)} %copy.33), calls=%async_computation.3 | async-start | bytes 1048576 | tf_op jit(solution)/shard_map/all_to_all | solution.py:14
  82.3 59.8 %all-reduce.3.cloned.1.call-start = ((), (), s32[]{:S(2)}) async-start(), calls=%async_computation.8 | async-start | bytes 2097152
  83.9 8.2 %copy-start.8 = (f32[512]{0:T(512)S(1)}, f32[512]{0:T(512)}, u32[]{:S(2)}) copy-start(f32[512]{0:T(512)} %param.9) | copy-start | bytes 6148
  85.9 84.8 %reduce-scatter.2.cloned.1.call-start = ((), (), s32[]{:S(2)}) async-start(), calls=%async_computation.5 | async-start | bytes 1310720 | tf_op jit(solution)/shard_map/reduce_scatter | solution.py:89
  92.1 3.1 %copy-start.9 = (u32[32]{0:T(128)S(1)}, u32[32]{0:T(128)}, u32[]{:S(2)}) copy-start(u32[32]{0:T(128)} %constant.33) | copy-start | bytes 388
  94.6 49.1 %copy-start.7 = (bf16[1,512,512]{2,1,0:T(8,128)(2,1)S(1)}, bf16[1,512,512]{2,1,0:T(8,128)(2,1)}, u32[]{:S(2)}) copy-start(bf16[1,512,512]{2,1,0:T(8,128)(2,1)} %param.11) | copy-start | bytes 1572868
  94.6 49.1 %copy-start.10 = (bf16[512,512]{1,0:T(8,128)(2,1)S(1)}, bf16[512,512]{1,0:T(8,128)(2,1)}, u32[]{:S(2)}) copy-start(bf16[512,512]{1,0:T(8,128)(2,1)} %get-tuple-element.19) | copy-start | bytes 1572868
  94.6 122.8 %all-gather.5.cloned.1.call-start = ((), (), s32[]{:S(2)}) async-start(), calls=%async_computation.6 | async-start | bytes 2621440 | tf_op jit(solution)/shard_map/all_gather | solution.py:19
Sparse Core Ops, SparseCore 0:
  9.6 48.6 all-gather.6
  86.3 55.7 all-reduce.2
  144.4 26.1 reduce-scatter.1
  172.7 44.5 all-gather.4
